TPU v7x, 128 devices: a whole 4x4x4 slice. The times are simulated.
128 devices in a mesh: pipe: 4 (over z_hi, core), expert: 32 (over x, z_lo, y).
Axes of the slice: x: 4, y: 4, z: 4 (z_hi: 2, z_lo: 2; z = z_hi * 2 + z_lo), core: 2. Of those that a mesh axis runs over, the one named last changes fastest.
Arguments:
- grad_out: bfloat16 [4, 2, 2048, 2048], P('pipe', None, 'expert'), may hold values from -6 to 6
- route_weights: float32 [4, 2, 2048, 8], P('pipe', None, 'expert'), may hold values from 0.1 to 0.6
- expert_ids: int32 [4, 2, 2048, 8], P('pipe', None, 'expert'), may hold values from 0 to 31, all different within a row; in each aligned block of 64 rows (0 to 63, 64 to 127, ..., all dimensions but the last counted through in order) at most 20 rows name the same one
- hot_pos: int32 [4, 8], P('pipe'), may hold values from 0 to 3, as said below
- up_weight: bfloat16 [4, 32, 2048, 768], P('pipe', 'expert'), may hold values from -0.125 to 0.125
- down_weight: bfloat16 [4, 32, 768, 2048], P('pipe', 'expert'), may hold values from -0.21875 to 0.21875
- saved_inputs: bfloat16 [4, 2, 32, 32, 25, 2048], P('pipe', None, 'expert'), may hold values from -6 to 6
- saved_gates: bfloat16 [4, 2, 32, 32, 25, 768], P('pipe', None, 'expert'), may hold values from -8 to 8
Outputs:
- sent_back: bfloat16 [4, 2, 2048, 2048], P('pipe', None, 'expert')
- up_grad: bfloat16 [4, 32, 2048, 768], P('pipe', 'expert')
- down_grad: bfloat16 [4, 32, 768, 2048], P('pipe', 'expert')
- gate_grads: bfloat16 [4, 2, 32, 32, 25, 768], P('pipe', None, 'expert')
- hot_up_grad: bfloat16 [4, 32, 512, 768], P('pipe', 'expert')
- hot_down_grad: bfloat16 [4, 32, 192, 2048], P('pipe', 'expert')
Inputs may be any that keep to these rules, and one draw needn't show every extreme that they name: `expert_ids`: each token names 8 different experts. Among the rows of one device in one micro-batch of one section no expert is named more than 20 times, a bound that some block reaches. `hot_pos`: in section 0 the first and the last group copy their expert 4 - 2; in section 1 the first group copies its expert 4 - 1 and the last group its expert 4 - 3.
All inputs are finite; a program needn't handle non-finite values.
Results may differ from a plain program's by a relative error of at most 0.0065.
Values may be sent and summed in bfloat16 or wider, within the bound.
No kernel may reach another device: no remote copies, remote signals or barrier semaphores. Data moves between devices by JAX's collectives and lax.ppermute only.
A program may use at most 192 MiB of HBM per device.

v0:
```python
import jax
import jax.numpy as jnp
from jax import lax
from jax.sharding import PartitionSpec as P

TOP = 8
REPL = 4
MB = 2


def partner(value, axis, bit):
    mask = 2**bit
    pairs = [(source, source ^ mask) for source in range(lax.axis_size(axis))]
    return lax.ppermute(value, axis, pairs)


def from_behind(block, axis, distance):
    devices = range(lax.axis_size(axis))
    route = [((i - distance) % len(devices), i) for i in devices]
    return lax.ppermute(block, axis, route)


def route_slots(expert_row, sender, hot_table, num_experts, most_rows, slot_count):
    onehot = (expert_row[:, None] == jnp.arange(num_experts, dtype=jnp.int32)[None, :]).astype(
        jnp.int32
    )
    order_pos = jnp.sum(jnp.cumsum(onehot, axis=0) * onehot, axis=1) - 1
    group_id = expert_row // REPL
    hot_count = hot_table.shape[0]
    owner_pos = jnp.sum(
        (group_id[:, None] == jnp.arange(hot_count, dtype=jnp.int32)[None, :]).astype(jnp.int32)
        * hot_table[None, :],
        axis=1,
    )
    is_hot = expert_row % REPL == owner_pos
    target = jnp.where(is_hot, REPL * group_id + (sender + order_pos) % REPL, expert_row)
    slot_pos = jnp.where(is_hot, most_rows + order_pos // REPL, order_pos)
    return target * slot_count + slot_pos


def expert_rows(grad_rows, input_rows, gate_rows, up_w, down_w):
    up_value = jnp.dot(input_rows, up_w, preferred_element_type=jnp.float32)
    gate_value = gate_rows.astype(jnp.float32)
    gate_sig = jax.nn.sigmoid(gate_value)
    active = gate_value * gate_sig
    hidden = (active * up_value).astype(jnp.bfloat16)
    grad_hidden = lax.dot_general(
        grad_rows, down_w, (((1,), (1,)), ((), ())), preferred_element_type=jnp.float32
    )
    grad_up = (grad_hidden * active).astype(jnp.bfloat16)
    grad_gate = (grad_hidden * up_value * gate_sig * (1.0 + gate_value * (1.0 - gate_sig))).astype(
        jnp.bfloat16
    )
    back_rows = lax.dot_general(
        grad_up, up_w, (((1,), (1,)), ((), ())), preferred_element_type=jnp.float32
    ).astype(jnp.bfloat16)
    down_term = lax.dot_general(
        hidden, grad_rows, (((0,), (0,)), ((), ())), preferred_element_type=jnp.float32
    )
    up_term = lax.dot_general(
        input_rows, grad_up, (((0,), (0,)), ((), ())), preferred_element_type=jnp.float32
    )
    return (back_rows, grad_gate, up_term, down_term)


def take_part(matrix, index, parts):
    length = matrix.shape[0] // parts
    return lax.dynamic_slice_in_dim(matrix, index * length, length, 0)


def per_device(
    grad_out, route_weights, expert_ids, hot_pos, up_weight, down_weight, saved_inputs, saved_gates
):
    experts = lax.axis_size("expert")
    device = lax.axis_index("expert")
    features = grad_out.shape[-1]
    hidden_units = saved_gates.shape[-1]
    token_count = grad_out.shape[2]
    slot_count = saved_inputs.shape[4]
    quarter_rows = slot_count // (REPL + 1)
    most_rows = REPL * quarter_rows
    hot_table = hot_pos[0]
    group_id = device // REPL
    local_pos = device % REPL
    low_bit = local_pos % 2
    high_bit = local_pos // 2
    owner_pos = jnp.sum(
        jnp.where(jnp.arange(hot_table.shape[0], dtype=jnp.int32) == group_id, hot_table, 0)
    )
    is_owner = local_pos == owner_pos
    own_up = up_weight[0, 0]
    own_down = down_weight[0, 0]
    owner_mask = is_owner.astype(jnp.bfloat16)
    masked = (own_up * owner_mask, own_down * owner_mask)
    from_low = partner((masked[0], masked[1]), "expert", 0)
    step_one = (masked[0] + from_low[0], masked[1] + from_low[1])
    second = partner((step_one[0], step_one[1]), "expert", 1)
    hot_up = step_one[0] + second[0]
    hot_down = step_one[1] + second[1]
    outputs = []
    token_grads = []
    for batch_idx in range(MB):
        expert_row = expert_ids[0, batch_idx].reshape(-1)
        token_flat_index = route_slots(
            expert_row, device, hot_table, experts, most_rows, slot_count
        )
        scaled = (
            route_weights[0, batch_idx][:, :, None]
            * grad_out[0, batch_idx][:, None, :].astype(jnp.float32)
        ).astype(jnp.bfloat16)
        routed_rows = scaled.reshape(-1, features)
        buffer = (
            jnp.zeros((experts * slot_count, features), jnp.bfloat16)
            .at[token_flat_index]
            .set(routed_rows)
        )
        flat_index, buffer = (token_flat_index, buffer.reshape(experts, slot_count, features))
        received = lax.all_to_all(buffer, "expert", split_axis=0, concat_axis=0, tiled=True)
        inputs_batch = saved_inputs[0, batch_idx, 0]
        gates_batch = saved_gates[0, batch_idx, 0]
        first_part = expert_rows(
            received[:, :most_rows].reshape(-1, features),
            inputs_batch[:, :most_rows].reshape(-1, features),
            gates_batch[:, :most_rows].reshape(-1, hidden_units),
            own_up,
            own_down,
        )
        expert_second = expert_rows(
            received[:, most_rows:].reshape(-1, features),
            inputs_batch[:, most_rows:].reshape(-1, features),
            gates_batch[:, most_rows:].reshape(-1, hidden_units),
            hot_up,
            hot_down,
        )
        back = jnp.concatenate(
            [
                first_part[0].reshape(experts, most_rows, features),
                expert_second[0].reshape(experts, quarter_rows, features),
            ],
            1,
        )
        gate_grad = jnp.concatenate(
            [
                first_part[1].reshape(experts, most_rows, hidden_units),
                expert_second[1].reshape(experts, quarter_rows, hidden_units),
            ],
            1,
        )
        results = (
            back,
            gate_grad,
            first_part[2],
            first_part[3],
            expert_second[2],
            expert_second[3],
        )
        outputs.append(results)
        returned = lax.all_to_all(results[0], "expert", split_axis=0, concat_axis=0, tiled=True)
        gathered = returned.reshape(experts * slot_count, features)[flat_index]
        summed = jnp.sum(gathered.reshape(token_count, TOP, features).astype(jnp.float32), axis=1)
        token_grads.append(
            (summed + grad_out[0, batch_idx].astype(jnp.float32)).astype(jnp.bfloat16)
        )
    own_up_sum = jnp.zeros((features, hidden_units), jnp.float32)
    own_down_sum = jnp.zeros((hidden_units, features), jnp.float32)
    rep_up_sum = jnp.zeros((features, hidden_units), jnp.float32)
    rep_down_sum = jnp.zeros((hidden_units, features), jnp.float32)
    for member in outputs:
        own_up_sum = own_up_sum + member[2]
        own_down_sum = own_down_sum + member[3]
        rep_up_sum = rep_up_sum + member[4]
        rep_down_sum = rep_down_sum + member[5]
    sent_back = from_behind(jnp.stack(token_grads, 0), "pipe", -1)
    rep_terms = (rep_up_sum.astype(jnp.bfloat16), rep_down_sum.astype(jnp.bfloat16))
    outgoing = (take_part(rep_terms[0], 1 - high_bit, 2), take_part(rep_terms[1], 1 - high_bit, 2))
    incoming = partner((outgoing[0], outgoing[1]), "expert", 1)
    halves = (
        take_part(rep_terms[0], high_bit, 2).astype(jnp.float32) + incoming[0].astype(jnp.float32),
        take_part(rep_terms[1], high_bit, 2).astype(jnp.float32) + incoming[1].astype(jnp.float32),
    )
    outgoing = (take_part(halves[0], 1 - low_bit, 2), take_part(halves[1], 1 - low_bit, 2))
    incoming = partner((outgoing[0], outgoing[1]), "expert", 0)
    hot_up_part = (take_part(halves[0], low_bit, 2) + incoming[0]).astype(jnp.bfloat16)
    hot_down_part = (take_part(halves[1], low_bit, 2) + incoming[1]).astype(jnp.bfloat16)
    up_grad = own_up_sum.astype(jnp.bfloat16)
    down_grad = own_down_sum.astype(jnp.bfloat16)
    gate_grads = jnp.stack([member[1] for member in outputs], 0)
    return (
        sent_back[None],
        up_grad[None, None],
        down_grad[None, None],
        gate_grads[None, :, None],
        hot_up_part[None, None],
        hot_down_part[None, None],
    )


def solution(mesh):
    return jax.shard_map(
        per_device,
        mesh=mesh,
        in_specs=(
            P("pipe", None, "expert", None),
            P("pipe", None, "expert", None),
            P("pipe", None, "expert", None),
            P("pipe", None),
            P("pipe", "expert", None, None),
            P("pipe", "expert", None, None),
            P("pipe", None, "expert", None, None, None),
            P("pipe", None, "expert", None, None, None),
        ),
        out_specs=(
            P("pipe", None, "expert", None),
            P("pipe", "expert", None, None),
            P("pipe", "expert", None, None),
            P("pipe", None, "expert", None, None, None),
            P("pipe", "expert", None, None),
            P("pipe", "expert", None, None),
        ),
        check_vma=False,
    )
```

profile of v0, /device:TPU:31, one launch (start us, length us, event | category | flops | bytes accessed | tf_op | source)
XLA Modules:
  0.0 668.6 jit_solution(7600676001211848532)
XLA Ops:
  17.2 8.4 %all-to-all-start.2 = ((bf16[32,25,2048]{2,1,0:T(8,128)(2,1)}), bf16[32,25,2048]{2,1,0:T(8,128)(2,1)}, u32[]{:S(2)}, u32[]{:S(2)}) async-start(bf16[32,25,2048]{2,1,0:T(8,128)(2,1)} %reshape.678), calls=%async_computation.2 | async-start | bytes 8388608 | tf_op jit(solution)/shard_map/all_to_all | solution.py:118
  32.9 5.5 slice_bitcast_fusion
  64.1 20.3 %all-to-all-done.2 = bf16[32,25,2048]{2,1,0:T(8,128)(2,1)} async-done(((bf16[32,25,2048]{2,1,0:T(8,128)(2,1)}), bf16[32,25,2048]{2,1,0:T(8,128)(2,1)}, u32[]{:S(2)}, u32[]{:S(2)}) %all-to-all-start.2) | async-done | bytes 3276832 | tf_op jit(solution)/shard_map/all_to_all | solution.py:118
  84.3 8.3 %all-to-all-start = ((bf16[32,25,2048]{2,1,0:T(8,128)(2,1)}), bf16[32,25,2048]{2,1,0:T(8,128)(2,1)}, u32[]{:S(2)}, u32[]{:S(2)}) async-start(bf16[32,25,2048]{2,1,0:T(8,128)(2,1)} %reshape.671), calls=%async_computation | async-start | bytes 8388608 | tf_op jit(solution)/shard_map/all_to_all | solution.py:118
  112.5 5.3 reshape.684
  117.8 5.4 fusion.2
  126.7 59.5 %collective-permute-done.2 = bf16[2048,768]{1,0:T(8,128)(2,1)} collective-permute-done((bf16[2048,768]{1,0:T(8,128)(2,1)}, bf16[2048,768]{1,0:T(8,128)(2,1)}, u32[]{:S(2)}, u32[]{:S(2)}) %collective-permute-start.2) | collective-permute-done | bytes 3145760 | tf_op jit(solution)/shard_map/ppermute | solution.py:14
  190.2 63.4 %collective-permute-done = bf16[768,2048]{1,0:T(8,128)(2,1)} collective-permute-done((bf16[768,2048]{1,0:T(8,128)(2,1)}, bf16[768,2048]{1,0:T(8,128)(2,1)}, u32[]{:S(2)}, u32[]{:S(2)}) %collective-permute-start) | collective-permute-done | bytes 3145760 | tf_op jit(solution)/shard_map/ppermute | solution.py:14
  281.4 6.8 %multiply_convert_fusion = (bf16[640,768]{1,0:T(8,128)(2,1)}, bf16[640,768]{1,0:T(8,128)(2,1)S(1)}) fusion(f32[640,768]{1,0:T(8,128)} %reshape.698, f32[640,768]{1,0:T(8,128)} %fusion.2, bf16[640,2048]{1,0:T(8,128)(2,1)} %reshape.679, bf16[1,1,768,2048]{3,2,1,0:T(8,128)(2,1)S(1)} %copy-done.1), kind=kOutput, calls=%fused_computation.45 | convolution fusion | flops 2019655680 | bytes 11665408 | tf_op jit(solution)/shard_map/dot_general | solution.py:47
  298.0 6.7 %multiply_convert_fusion.1 = (bf16[640,768]{1,0:T(8,128)(2,1)}, bf16[640,768]{1,0:T(8,128)(2,1)S(1)}) fusion(f32[640,768]{1,0:T(8,128)} %reshape.693, f32[640,768]{1,0:T(8,128)} %fusion.4, bf16[640,2048]{1,0:T(8,128)(2,1)} %reshape.672, bf16[1,1,768,2048]{3,2,1,0:T(8,128)(2,1)S(1)} %copy-done.1), kind=kOutput, calls=%fused_computation.46 | convolution fusion | flops 2019655680 | bytes 11665408 | tf_op jit(solution)/shard_map/dot_general | solution.py:47
  316.9 6.2 collective-permute-done.3
  327.5 63.0 %collective-permute-done.1 = bf16[768,2048]{1,0:T(8,128)(2,1)} collective-permute-done((bf16[768,2048]{1,0:T(8,128)(2,1)}, bf16[768,2048]{1,0:T(8,128)(2,1)}, u32[]{:S(2)}, u32[]{:S(2)}) %collective-permute-start.1) | collective-permute-done | bytes 3145760 | tf_op jit(solution)/shard_map/ppermute | solution.py:14
  399.6 5.3 pad_maximum_fusion.1
  404.9 15.8 %all-to-all-start.3 = ((bf16[32,25,2048]{2,1,0:T(8,128)(2,1)}), bf16[32,25,2048]{2,1,0:T(8,128)(2,1)}, u32[]{:S(2)}, u32[]{:S(2)}) async-start(bf16[32,25,2048]{2,1,0:T(8,128)(2,1)} %pad_maximum_fusion.1), calls=%async_computation.3 | async-start | bytes 8388608 | tf_op jit(solution)/shard_map/all_to_all | solution.py:158
  420.8 5.9 convolution_convert_fusion.1
  471.1 11.1 %all-to-all-done.3 = bf16[32,25,2048]{2,1,0:T(8,128)(2,1)} async-done(((bf16[32,25,2048]{2,1,0:T(8,128)(2,1)}), bf16[32,25,2048]{2,1,0:T(8,128)(2,1)}, u32[]{:S(2)}, u32[]{:S(2)}) %all-to-all-start.3) | async-done | bytes 3276832 | tf_op jit(solution)/shard_map/all_to_all | solution.py:158
  482.2 6.3 all-to-all-start.1
  495.5 6.3 fusion.13
  508.1 33.6 %collective-permute-done.5 = bf16[1024,768]{0,1:T(8,128)(2,1)} collective-permute-done((bf16[1024,768]{0,1:T(8,128)(2,1)}, bf16[1024,768]{0,1:T(8,128)(2,1)}, u32[]{:S(2)}, u32[]{:S(2)}) %collective-permute-start.5) | collective-permute-done | bytes 1572896 | tf_op jit(solution)/shard_map/ppermute | solution.py:14
  545.1 9.3 %collective-permute-start.6 = (f32[512,768]{0,1:T(8,128)}, f32[512,768]{0,1:T(8,128)}, u32[]{:S(2)}, u32[]{:S(2)}) collective-permute-start(f32[512,768]{0,1:T(8,128)} %constant_dynamic-slice_fusion.2), channel_id=1, source_target_pairs={{0,1},{1,0},{2,3},{3,2},{4,5},{5,4},{6,7},{7,6},{8,9},{9,8},{10,11... | collective-permute-start | bytes 4718600 | tf_op jit(solution)/shard_map/ppermute | solution.py:14
  554.4 32.4 %collective-permute-done.7 = bf16[384,2048]{1,0:T(8,128)(2,1)} collective-permute-done((bf16[384,2048]{1,0:T(8,128)(2,1)}, bf16[384,2048]{1,0:T(8,128)(2,1)}, u32[]{:S(2)}, u32[]{:S(2)}) %collective-permute-start.7) | collective-permute-done | bytes 1572896 | tf_op jit(solution)/shard_map/ppermute | solution.py:14
  590.9 9.1 %collective-permute-start.8 = (f32[192,2048]{1,0:T(8,128)}, f32[192,2048]{1,0:T(8,128)}, u32[]{:S(2)}, u32[]{:S(2)}) collective-permute-start(f32[192,2048]{1,0:T(8,128)} %constant_dynamic-slice_fusion), channel_id=1, source_target_pairs={{0,1},{1,0},{2,3},{3,2},{4,5},{5,4},{6,7},{7,6},{8,9},{9,8},{10,11... | collective-permute-start | bytes 4718600 | tf_op jit(solution)/shard_map/ppermute | solution.py:14
  623.2 7.2 %collective-permute-done.6 = f32[512,768]{0,1:T(8,128)} collective-permute-done((f32[512,768]{0,1:T(8,128)}, f32[512,768]{0,1:T(8,128)}, u32[]{:S(2)}, u32[]{:S(2)}) %collective-permute-start.6) | collective-permute-done | bytes 1572896 | tf_op jit(solution)/shard_map/ppermute | solution.py:14
  635.2 28.8 %collective-permute-done.8 = f32[192,2048]{1,0:T(8,128)} collective-permute-done((f32[192,2048]{1,0:T(8,128)}, f32[192,2048]{1,0:T(8,128)}, u32[]{:S(2)}, u32[]{:S(2)}) %collective-permute-start.8) | collective-permute-done | bytes 1572896 | tf_op jit(solution)/shard_map/ppermute | solution.py:14
  (212 shorter events, 236.5 us)
Async XLA Ops:
  17.2 9.7 %copy-start.2 = (bf16[1,1,2048,768]{3,2,1,0:T(8,128)(2,1)S(1)}, bf16[1,1,2048,768]{3,2,1,0:T(8,128)(2,1)}, u32[]{:S(2)}) copy-start(bf16[1,1,2048,768]{3,2,1,0:T(8,128)(2,1)} %param.12) | copy-start | bytes 9437188
  17.2 67.1 %all-to-all-start.2 = ((bf16[32,25,2048]{2,1,0:T(8,128)(2,1)}), bf16[32,25,2048]{2,1,0:T(8,128)(2,1)}, u32[]{:S(2)}, u32[]{:S(2)}) async-start(bf16[32,25,2048]{2,1,0:T(8,128)(2,1)} %reshape.678), calls=%async_computation.2 | async-start | bytes 8388608 | tf_op jit(solution)/shard_map/all_to_all | solution.py:118
  28.8 157.3 %collective-permute-start.2 = (bf16[2048,768]{1,0:T(8,128)(2,1)}, bf16[2048,768]{1,0:T(8,128)(2,1)}, u32[]{:S(2)}, u32[]{:S(2)}) collective-permute-start(bf16[2048,768]{1,0:T(8,128)(2,1)} %bitcast_multiply_fusion.2), channel_id=1, source_target_pairs={{0,1},{1,0},{2,3},{3,2},{4,5},{5,4},{6,7},{7,6},{8,9},{9,8},{10,11... | collective-permute-start | bytes 9437192 | tf_op jit(solution)/shard_map/ppermute | solution.py:14
  31.9 221.7 %collective-permute-start = (bf16[768,2048]{1,0:T(8,128)(2,1)}, bf16[768,2048]{1,0:T(8,128)(2,1)}, u32[]{:S(2)}, u32[]{:S(2)}) collective-permute-start(bf16[768,2048]{1,0:T(8,128)(2,1)} %bitcast_multiply_fusion.3), channel_id=1, source_target_pairs={{0,1},{1,0},{2,3},{3,2},{4,5},{5,4},{6,7},{7,6},{8,9},{9,8},{10,11... | collective-permute-start | bytes 9437192 | tf_op jit(solution)/shard_map/ppermute | solution.py:14
  84.3 187.9 %all-to-all-start = ((bf16[32,25,2048]{2,1,0:T(8,128)(2,1)}), bf16[32,25,2048]{2,1,0:T(8,128)(2,1)}, u32[]{:S(2)}, u32[]{:S(2)}) async-start(bf16[32,25,2048]{2,1,0:T(8,128)(2,1)} %reshape.671), calls=%async_computation | async-start | bytes 8388608 | tf_op jit(solution)/shard_map/all_to_all | solution.py:118
  123.2 63.0 %copy-start.4 = (bf16[1,1,2048,768]{3,2,1,0:T(8,128)(2,1)S(1)}, bf16[1,1,2048,768]{3,2,1,0:T(8,128)(2,1)}, u32[]{:S(2)}) copy-start(bf16[1,1,2048,768]{3,2,1,0:T(8,128)(2,1)} %param.12) | copy-start | bytes 9437188
  126.7 126.9 %copy-start.1 = (bf16[1,1,768,2048]{3,2,1,0:T(8,128)(2,1)S(1)}, bf16[1,1,768,2048]{3,2,1,0:T(8,128)(2,1)}, u32[]{:S(2)}) copy-start(bf16[1,1,768,2048]{3,2,1,0:T(8,128)(2,1)} %param.13) | copy-start | bytes 9437188
  190.2 132.9 %collective-permute-start.3 = (bf16[2048,768]{1,0:T(8,128)(2,1)}, bf16[2048,768]{1,0:T(8,128)(2,1)}, u32[]{:S(2)}, u32[]{:S(2)}) collective-permute-start(bf16[2048,768]{1,0:T(8,128)(2,1)} %fusion.100), channel_id=1, source_target_pairs={{0,2},{1,3},{2,0},{3,1},{4,6},{5,7},{6,4},{7,5},{8,10},{9,11},{10,... | collective-permute-start | bytes 9437192 | tf_op jit(solution)/shard_map/ppermute | solution.py:14
  257.5 133.0 %collective-permute-start.1 = (bf16[768,2048]{1,0:T(8,128)(2,1)}, bf16[768,2048]{1,0:T(8,128)(2,1)}, u32[]{:S(2)}, u32[]{:S(2)}) collective-permute-start(bf16[768,2048]{1,0:T(8,128)(2,1)} %fusion.99), channel_id=1, source_target_pairs={{0,2},{1,3},{2,0},{3,1},{4,6},{5,7},{6,4},{7,5},{8,10},{9,11},{10,... | collective-permute-start | bytes 9437192 | tf_op jit(solution)/shard_map/ppermute | solution.py:14
  316.8 9.9 %copy-start.17 = (bf16[160,2048]{1,0:T(8,128)(2,1)S(1)}, bf16[160,2048]{1,0:T(8,128)(2,1)}, u32[]{:S(2)}) copy-start(bf16[160,2048]{1,0:T(8,128)(2,1)} %reshape.690) | copy-start | bytes 1966084
  326.7 63.8 %copy-start.28 = (bf16[160,2048]{1,0:T(8,128)(2,1)S(1)}, bf16[160,2048]{1,0:T(8,128)(2,1)}, u32[]{:S(2)}) copy-start(bf16[160,2048]{1,0:T(8,128)(2,1)} %reshape.681) | copy-start | bytes 1966084
  326.7 63.8 %copy-start.32 = (f32[160,768]{1,0:T(8,128)S(1)}, f32[160,768]{1,0:T(8,128)}, u32[]{:S(2)}) copy-start(f32[160,768]{1,0:T(8,128)} %reshape.699) | copy-start | bytes 1474564
  327.5 68.0 %copy-start.33 = (f32[160,768]{1,0:T(8,128)}, f32[160,768]{1,0:T(8,128)S(1)}, u32[]{:S(2)}) copy-start(f32[160,768]{1,0:T(8,128)S(1)} %convolution_bitcast_fusion) | copy-start | bytes 1474564
  404.9 77.3 %all-to-all-start.3 = ((bf16[32,25,2048]{2,1,0:T(8,128)(2,1)}), bf16[32,25,2048]{2,1,0:T(8,128)(2,1)}, u32[]{:S(2)}, u32[]{:S(2)}) async-start(bf16[32,25,2048]{2,1,0:T(8,128)(2,1)} %pad_maximum_fusion.1), calls=%async_computation.3 | async-start | bytes 8388608 | tf_op jit(solution)/shard_map/all_to_all | solution.py:158
  457.9 83.8 %collective-permute-start.5 = (bf16[1024,768]{0,1:T(8,128)(2,1)}, bf16[1024,768]{0,1:T(8,128)(2,1)}, u32[]{:S(2)}, u32[]{:S(2)}) collective-permute-start(bf16[1024,768]{0,1:T(8,128)(2,1)} %dynamic-slice_bitcast_fusion), channel_id=1, source_target_pairs={{0,2},{1,3},{2,0},{3,1},{4,6},{5,7},{6,4},{7,5},{8,10},{9,11},{10,... | collective-permute-start | bytes 4718600 | tf_op jit(solution)/shard_map/ppermute | solution.py:14
  482.2 127.8 %all-to-all-start.1 = ((bf16[32,25,2048]{2,1,0:T(8,128)(2,1)}), bf16[32,25,2048]{2,1,0:T(8,128)(2,1)}, u32[]{:S(2)}, u32[]{:S(2)}) async-start(bf16[32,25,2048]{2,1,0:T(8,128)(2,1)} %pad_maximum_fusion), calls=%async_computation.1 | async-start | bytes 8388608 | tf_op jit(solution)/shard_map/all_to_all | solution.py:158
  494.3 92.5 %collective-permute-start.7 = (bf16[384,2048]{1,0:T(8,128)(2,1)}, bf16[384,2048]{1,0:T(8,128)(2,1)}, u32[]{:S(2)}, u32[]{:S(2)}) collective-permute-start(bf16[384,2048]{1,0:T(8,128)(2,1)} %constant_dynamic-slice_fusion.1), channel_id=1, source_target_pairs={{0,2},{1,3},{2,0},{3,1},{4,6},{5,7},{6,4},{7,5},{8,10},{9,11},{10,... | collective-permute-start | bytes 4718600 | tf_op jit(solution)/shard_map/ppermute | solution.py:14
  504.6 37.0 %copy-start.11 = (bf16[768,2048]{1,0:T(8,128)(2,1)S(1)}, bf16[768,2048]{1,0:T(8,128)(2,1)}, u32[]{:S(2)}) copy-start(bf16[768,2048]{1,0:T(8,128)(2,1)} %copy-done.10) | copy-start | bytes 9437188
  543.7 45.1 %copy-start.6 = (f32[1024,768]{0,1:T(8,128)}, f32[1024,768]{0,1:T(8,128)S(1)}, u32[]{:S(2)}) copy-start(f32[1024,768]{0,1:T(8,128)S(1)} %bitcast_add_fusion) | copy-start | bytes 9437188
  545.1 85.2 %collective-permute-start.6 = (f32[512,768]{0,1:T(8,128)}, f32[512,768]{0,1:T(8,128)}, u32[]{:S(2)}, u32[]{:S(2)}) collective-permute-start(f32[512,768]{0,1:T(8,128)} %constant_dynamic-slice_fusion.2), channel_id=1, source_target_pairs={{0,1},{1,0},{2,3},{3,2},{4,5},{5,4},{6,7},{7,6},{8,9},{9,8},{10,11... | collective-permute-start | bytes 4718600 | tf_op jit(solution)/shard_map/ppermute | solution.py:14
  590.9 73.1 %collective-permute-start.8 = (f32[192,2048]{1,0:T(8,128)}, f32[192,2048]{1,0:T(8,128)}, u32[]{:S(2)}, u32[]{:S(2)}) collective-permute-start(f32[192,2048]{1,0:T(8,128)} %constant_dynamic-slice_fusion), channel_id=1, source_target_pairs={{0,1},{1,0},{2,3},{3,2},{4,5},{5,4},{6,7},{7,6},{8,9},{9,8},{10,11... | collective-permute-start | bytes 4718600 | tf_op jit(solution)/shard_map/ppermute | solution.py:14
  619.9 10.4 %copy-start.7 = (f32[1024,768]{0,1:T(8,128)S(1)}, f32[1024,768]{0,1:T(8,128)}, u32[]{:S(2)}) copy-start(f32[1024,768]{0,1:T(8,128)} %copy-done.6) | copy-start | bytes 9437188
  621.4 42.6 %copy-start.9 = (f32[384,2048]{1,0:T(8,128)S(1)}, f32[384,2048]{1,0:T(8,128)}, u32[]{:S(2)}) copy-start(f32[384,2048]{1,0:T(8,128)} %copy-done.8) | copy-start | bytes 9437188
  622.3 44.2 %collective-permute-start.4 = (bf16[2,64,2048]{2,1,0:T(8,128)(2,1)}, bf16[2,64,2048]{2,1,0:T(8,128)(2,1)}, u32[]{:S(2)}, u32[]{:S(2)}) collective-permute-start(bf16[2,64,2048]{2,1,0:T(8,128)(2,1)} %pad_maximum_fusion.2), channel_id=1, source_target_pairs={{32,0},{64,32},{96,64},{0,96},{33,1},{65,33},{97,65},{1,97},{34,2}... | collective-permute-start | bytes 1572872 | tf_op jit(solution)/shard_map/ppermute | solution.py:20
  (29 other events, 119.3 us)
where the time goes:
time: 676 us; the launch traced here: 669 us
  waiting for transfers between devices  326 us (48%)
  local copies, waits for them, and re-layouts  139 us (21%)
  matrix products  76.5 us (11%)
  other arithmetic  63 us (9%)
  starting transfers between devices  62.4 us (9%)
    ppermute x8, waiting for transfers between devices, partner(): return lax.ppermute(value, axis, pairs)  294 us
    dot_general x4, matrix products, expert_rows(): lax.dot_general(grad_rows, down_w, (((1,), (1,)), ((), ())), preferred_el...  23.5 us
    ppermute x8, starting transfers between devices, partner(): return lax.ppermute(value, axis, pairs)  22.7 us
    all_to_all x2, starting transfers between devices, per_device(): lax.all_to_all(results[0], 'expert', split_axis=0, concat_axis=0, tiled=T...  22.2 us
    all_to_all x2, waiting for transfers between devices, per_device(): lax.all_to_all(buffer, 'expert', split_axis=0, concat_axis=0, tiled=True)  20.3 us
    dot_general x4, matrix products, expert_rows(): lax.dot_general(hidden, grad_rows, (((0,), (0,)), ((), ())), preferred_el...  19.1 us
    all_to_all x2, starting transfers between devices, per_device(): lax.all_to_all(buffer, 'expert', split_axis=0, concat_axis=0, tiled=True)  16.7 us
    unnamed x84, local copies, waits for them, and re-layouts  16.2 us
  transfers between devices with their start and end apart: 13, of which 10 were waited for; matrix products, arithmetic and copies ran while one was open for 36% of the time, Pallas kernels for 0%

commit v1 on v0

--- a/solution.py
+++ b/solution.py
@@ -71,8 +71,8 @@
 def per_device(
     grad_out, route_weights, expert_ids, hot_pos, up_weight, down_weight, saved_inputs, saved_gates
 ):
-    experts = lax.axis_size("expert")
-    device = lax.axis_index("expert")
+    experts = lax.axis_size("grp") * lax.axis_size("j")
+    device = lax.axis_index("grp") * lax.axis_size("j") + lax.axis_index("j")
     features = grad_out.shape[-1]
     hidden_units = saved_gates.shape[-1]
     token_count = grad_out.shape[2]
@@ -82,8 +82,6 @@
     hot_table = hot_pos[0]
     group_id = device // REPL
     local_pos = device % REPL
-    low_bit = local_pos % 2
-    high_bit = local_pos // 2
     owner_pos = jnp.sum(
         jnp.where(jnp.arange(hot_table.shape[0], dtype=jnp.int32) == group_id, hot_table, 0)
     )
@@ -91,12 +89,7 @@
     own_up = up_weight[0, 0]
     own_down = down_weight[0, 0]
     owner_mask = is_owner.astype(jnp.bfloat16)
-    masked = (own_up * owner_mask, own_down * owner_mask)
-    from_low = partner((masked[0], masked[1]), "expert", 0)
-    step_one = (masked[0] + from_low[0], masked[1] + from_low[1])
-    second = partner((step_one[0], step_one[1]), "expert", 1)
-    hot_up = step_one[0] + second[0]
-    hot_down = step_one[1] + second[1]
+    hot_up, hot_down = lax.psum((own_up * owner_mask, own_down * owner_mask), "j")
     outputs = []
     token_grads = []
     for batch_idx in range(MB):
@@ -115,7 +108,7 @@
             .set(routed_rows)
         )
         flat_index, buffer = (token_flat_index, buffer.reshape(experts, slot_count, features))
-        received = lax.all_to_all(buffer, "expert", split_axis=0, concat_axis=0, tiled=True)
+        received = lax.all_to_all(buffer, ("grp", "j"), split_axis=0, concat_axis=0, tiled=True)
         inputs_batch = saved_inputs[0, batch_idx, 0]
         gates_batch = saved_gates[0, batch_idx, 0]
         first_part = expert_rows(
@@ -155,7 +148,7 @@
             expert_second[3],
         )
         outputs.append(results)
-        returned = lax.all_to_all(results[0], "expert", split_axis=0, concat_axis=0, tiled=True)
+        returned = lax.all_to_all(results[0], ("grp", "j"), split_axis=0, concat_axis=0, tiled=True)
         gathered = returned.reshape(experts * slot_count, features)[flat_index]
         summed = jnp.sum(gathered.reshape(token_count, TOP, features).astype(jnp.float32), axis=1)
         token_grads.append(
@@ -171,17 +164,13 @@
         rep_up_sum = rep_up_sum + member[4]
         rep_down_sum = rep_down_sum + member[5]
     sent_back = from_behind(jnp.stack(token_grads, 0), "pipe", -1)
-    rep_terms = (rep_up_sum.astype(jnp.bfloat16), rep_down_sum.astype(jnp.bfloat16))
-    outgoing = (take_part(rep_terms[0], 1 - high_bit, 2), take_part(rep_terms[1], 1 - high_bit, 2))
-    incoming = partner((outgoing[0], outgoing[1]), "expert", 1)
-    halves = (
-        take_part(rep_terms[0], high_bit, 2).astype(jnp.float32) + incoming[0].astype(jnp.float32),
-        take_part(rep_terms[1], high_bit, 2).astype(jnp.float32) + incoming[1].astype(jnp.float32),
-    )
-    outgoing = (take_part(halves[0], 1 - low_bit, 2), take_part(halves[1], 1 - low_bit, 2))
-    incoming = partner((outgoing[0], outgoing[1]), "expert", 0)
-    hot_up_part = (take_part(halves[0], low_bit, 2) + incoming[0]).astype(jnp.bfloat16)
-    hot_down_part = (take_part(halves[1], low_bit, 2) + incoming[1]).astype(jnp.bfloat16)
+    rep_terms = (
+        rep_up_sum.astype(jnp.bfloat16).astype(jnp.float32),
+        rep_down_sum.astype(jnp.bfloat16).astype(jnp.float32),
+    )
+    hot_up_part, hot_down_part = lax.psum_scatter(rep_terms, "j", scatter_dimension=0, tiled=True)
+    hot_up_part = hot_up_part.astype(jnp.bfloat16)
+    hot_down_part = hot_down_part.astype(jnp.bfloat16)
     up_grad = own_up_sum.astype(jnp.bfloat16)
     down_grad = own_down_sum.astype(jnp.bfloat16)
     gate_grads = jnp.stack([member[1] for member in outputs], 0)
@@ -195,27 +184,32 @@
     )
 
 
+EXPERT = ("grp", "j")
+
+
 def solution(mesh):
+    groups = mesh.devices.reshape(mesh.shape["pipe"], -1, REPL)
+    group_mesh = jax.sharding.Mesh(groups, ("pipe", "grp", "j"))
     return jax.shard_map(
         per_device,
-        mesh=mesh,
+        mesh=group_mesh,
         in_specs=(
-            P("pipe", None, "expert", None),
-            P("pipe", None, "expert", None),
-            P("pipe", None, "expert", None),
+            P("pipe", None, EXPERT, None),
+            P("pipe", None, EXPERT, None),
+            P("pipe", None, EXPERT, None),
             P("pipe", None),
-            P("pipe", "expert", None, None),
-            P("pipe", "expert", None, None),
-            P("pipe", None, "expert", None, None, None),
-            P("pipe", None, "expert", None, None, None),
+            P("pipe", EXPERT, None, None),
+            P("pipe", EXPERT, None, None),
+            P("pipe", None, EXPERT, None, None, None),
+            P("pipe", None, EXPERT, None, None, None),
         ),
         out_specs=(
-            P("pipe", None, "expert", None),
-            P("pipe", "expert", None, None),
-            P("pipe", "expert", None, None),
-            P("pipe", None, "expert", None, None, None),
-            P("pipe", "expert", None, None),
-            P("pipe", "expert", None, None),
+            P("pipe", None, EXPERT, None),
+            P("pipe", EXPERT, None, None),
+            P("pipe", EXPERT, None, None),
+            P("pipe", None, EXPERT, None, None, None),
+            P("pipe", EXPERT, None, None),
+            P("pipe", EXPERT, None, None),
         ),
         check_vma=False,
     )

time: 676 us -> 540 us (0.80)
  the two profiles are of different devices: /device:TPU:31 before, /device:TPU:15 now
where the time goes in v1:
time: 540 us; the launch traced here: 533 us
  waiting for transfers between devices  220 us (41%)
  local copies, waits for them, and re-layouts  132 us (24%)
  matrix products  78.7 us (15%)
  starting transfers between devices  43.4 us (8%)
  other arithmetic  42.9 us (8%)
  between operations  15.3 us (3%)
    all_to_all x2, waiting for transfers between devices, per_device(): lax.all_to_all(buffer, ('grp', 'j'), split_axis=0, concat_axis=0, tiled=T...  89.1 us
    psum x1, waiting for transfers between devices, per_device(): lax.psum((own_up * owner_mask, own_down * owner_mask), 'j')  85.6 us
    all_to_all x2, waiting for transfers between devices, per_device(): lax.all_to_all(results[0], ('grp', 'j'), split_axis=0, concat_axis=0, til...  45.2 us
    unnamed x94, local copies, waits for them, and re-layouts  19.6 us
    dot_general x4, matrix products, expert_rows(): lax.dot_general(grad_rows, down_w, (((1,), (1,)), ((), ())), preferred_el...  19.5 us
    all_to_all x2, starting transfers between devices, per_device(): lax.all_to_all(buffer, ('grp', 'j'), split_axis=0, concat_axis=0, tiled=T...  17.9 us
    slice x4, local copies, waits for them, and re-layouts, per_device(): inputs_batch[:, :most_rows].reshape(-1, features)  17.3 us
    dot_general x4, matrix products, expert_rows(): up_value = jnp.dot(input_rows, up_w, preferred_element_type=jnp.float32)  17.2 us
  transfers between devices with their start and end apart: 8, of which 5 were waited for; matrix products, arithmetic and copies ran while one was open for 40% of the time, Pallas kernels for 0%

profile of v1, /device:TPU:15, one launch (start us, length us, event | category | flops | bytes accessed | tf_op | source)
XLA Modules:
  0.0 532.7 jit_solution(17326901988790741100)
XLA Ops:
  14.9 5.2 scatter_custom_fusion
  23.2 8.6 %all-to-all-start = ((bf16[32,25,2048]{2,1,0:T(8,128)(2,1)}), bf16[32,25,2048]{2,1,0:T(8,128)(2,1)}, u32[]{:S(2)}, u32[]{:S(2)}) async-start(bf16[32,25,2048]{2,1,0:T(8,128)(2,1)} %reshape.671), calls=%async_computation | async-start | bytes 8388608 | tf_op jit(solution)/shard_map/all_to_all | solution.py:111
  38.3 5.5 %scatter_custom_fusion.1 = bf16[800,2048]{1,0:T(8,128)(2,1)S(1)} fusion(s32[512]{0:T(512)S(1)} %bitcast.173, f32[64,2048]{1,0:T(8,128)} %get-tuple-element.43, f32[512]{0:T(512)S(1)} %mul.221, bf16[]{:T(256)} %constant.100.clone.1), kind=kCustom, calls=%fused_computation.40 | custom fusion | flops 2097152 | bytes 3803138 | tf_op jit(solution)/shard_map/scatter | solution.py:108
  46.6 45.7 %all-to-all-done = bf16[32,25,2048]{2,1,0:T(8,128)(2,1)} async-done(((bf16[32,25,2048]{2,1,0:T(8,128)(2,1)}), bf16[32,25,2048]{2,1,0:T(8,128)(2,1)}, u32[]{:S(2)}, u32[]{:S(2)}) %all-to-all-start) | async-done | bytes 3276832 | tf_op jit(solution)/shard_map/all_to_all | solution.py:111
  92.3 9.3 %all-to-all-start.2 = ((bf16[32,25,2048]{2,1,0:T(8,128)(2,1)}), bf16[32,25,2048]{2,1,0:T(8,128)(2,1)}, u32[]{:S(2)}, u32[]{:S(2)}) async-start(bf16[32,25,2048]{2,1,0:T(8,128)(2,1)} %reshape.678), calls=%async_computation.2 | async-start | bytes 8388608 | tf_op jit(solution)/shard_map/all_to_all | solution.py:111
  121.4 43.4 %all-to-all-done.2 = bf16[32,25,2048]{2,1,0:T(8,128)(2,1)} async-done(((bf16[32,25,2048]{2,1,0:T(8,128)(2,1)}), bf16[32,25,2048]{2,1,0:T(8,128)(2,1)}, u32[]{:S(2)}, u32[]{:S(2)}) %all-to-all-start.2) | async-done | bytes 3276832 | tf_op jit(solution)/shard_map/all_to_all | solution.py:111
  167.9 85.6 %all-reduce.3.cloned.1.call-done = (bf16[768,2048]{1,0:T(8,128)(2,1)}, bf16[2048,768]{1,0:T(8,128)(2,1)}) async-done(((bf16[768,2048]{1,0:T(8,128)(2,1)}, bf16[2048,768]{1,0:T(8,128)(2,1)}), (bf16[768,2048]{1,0:T(8,128)(2,1)}, bf16[2048,768]{1,0:T(8,128)(2,1)})) %all-reduce.3.cloned.1.call-update) | async-done | bytes 6291472 | tf_op jit(solution)/shard_map/psum | solution.py:92
  268.8 10.0 %reduce-scatter.5.cloned.1.call-start = ((), (), s32[]{:S(2)}) async-start(), calls=%async_computation.7 | async-start | bytes 7864320 | tf_op jit(solution)/shard_map/reduce_scatter | solution.py:171
  301.2 5.2 reshape.684
  306.4 6.2 %fusion.5 = f32[640,768]{1,0:T(8,128)} fusion(bf16[640,2048]{1,0:T(8,128)(2,1)} %reshape.684, bf16[1,1,2048,768]{3,2,1,0:T(8,128)(2,1)} %param.12), kind=kOutput, calls=%fused_computation.25 | convolution fusion | flops 2013265920 | bytes 7733248 | tf_op jit(solution)/shard_map/dot_general | solution.py:42
  316.6 5.2 reshape.672
  321.8 7.8 %multiply_convert_fusion.1 = (bf16[640,768]{1,0:T(8,128)(2,1)}, bf16[640,768]{1,0:T(8,128)(2,1)S(1)}) fusion(f32[640,768]{1,0:T(8,128)} %reshape.693, f32[640,768]{1,0:T(8,128)} %fusion.5, bf16[640,2048]{1,0:T(8,128)(2,1)} %reshape.672, bf16[1,1,768,2048]{3,2,1,0:T(8,128)(2,1)} %param.13), kind=kOutput, calls=%fused_computation.46 | convolution fusion | flops 2019655680 | bytes 11665408 | tf_op jit(solution)/shard_map/dot_general | solution.py:47
  334.3 5.1 reshape.673
  343.6 5.9 %pad_maximum_fusion = bf16[32,25,2048]{2,1,0:T(8,128)(2,1)} fusion(bf16[32,5,2048]{2,1,0:T(8,128)(2,1)} %reshape.675, bf16[32,20,2048]{2,1,0:T(8,128)(2,1)} %reshape.673), kind=kLoop, calls=%fused_computation.9 | loop fusion | flops 6553600 | bytes 6553600 | tf_op jit(solution)/shard_map/concatenate | solution.py:128
  349.5 8.0 %all-to-all-start.1 = ((bf16[32,25,2048]{2,1,0:T(8,128)(2,1)}), bf16[32,25,2048]{2,1,0:T(8,128)(2,1)}, u32[]{:S(2)}, u32[]{:S(2)}) async-start(bf16[32,25,2048]{2,1,0:T(8,128)(2,1)} %pad_maximum_fusion), calls=%async_computation.1 | async-start | bytes 8388608 | tf_op jit(solution)/shard_map/all_to_all | solution.py:151
  371.3 5.2 reshape.685
  376.5 6.1 %fusion.3 = f32[640,768]{1,0:T(8,128)} fusion(bf16[640,2048]{1,0:T(8,128)(2,1)} %reshape.685, bf16[1,1,2048,768]{3,2,1,0:T(8,128)(2,1)} %param.12), kind=kOutput, calls=%fused_computation.23 | convolution fusion | flops 2013265920 | bytes 7733248 | tf_op jit(solution)/shard_map/dot_general | solution.py:42
  386.6 5.2 reshape.679
  391.8 7.7 %multiply_convert_fusion = (bf16[640,768]{1,0:T(8,128)(2,1)}, bf16[640,768]{1,0:T(8,128)(2,1)S(1)}) fusion(f32[640,768]{1,0:T(8,128)} %reshape.698, f32[640,768]{1,0:T(8,128)} %fusion.3, bf16[640,2048]{1,0:T(8,128)(2,1)} %reshape.679, bf16[1,1,768,2048]{3,2,1,0:T(8,128)(2,1)} %param.13), kind=kOutput, calls=%fused_computation.45 | convolution fusion | flops 2019655680 | bytes 11665408 | tf_op jit(solution)/shard_map/dot_general | solution.py:47
  404.2 5.2 reshape.680
  420.3 6.3 %all-to-all-start.3 = ((bf16[32,25,2048]{2,1,0:T(8,128)(2,1)}), bf16[32,25,2048]{2,1,0:T(8,128)(2,1)}, u32[]{:S(2)}, u32[]{:S(2)}) async-start(bf16[32,25,2048]{2,1,0:T(8,128)(2,1)} %pad_maximum_fusion.1), calls=%async_computation.3 | async-start | bytes 8388608 | tf_op jit(solution)/shard_map/all_to_all | solution.py:151
  426.7 5.9 %fusion.64 = f32[768,2048]{1,0:T(8,128)} fusion(bf16[640,768]{1,0:T(8,128)(2,1)} %copy-done.34, bf16[640,2048]{1,0:T(8,128)(2,1)S(1)} %copy-done.3), kind=kOutput, calls=%fused_computation.170 | convolution fusion | flops 2013265920 | bytes 9895936 | tf_op jit(solution)/shard_map/dot_general | solution.py:60
  446.5 42.7 %all-to-all-done.3 = bf16[32,25,2048]{2,1,0:T(8,128)(2,1)} async-done(((bf16[32,25,2048]{2,1,0:T(8,128)(2,1)}), bf16[32,25,2048]{2,1,0:T(8,128)(2,1)}, u32[]{:S(2)}, u32[]{:S(2)}) %all-to-all-start.3) | async-done | bytes 3276832 | tf_op jit(solution)/shard_map/all_to_all | solution.py:151
  502.7 6.2 %fusion.13 = bf16[1,1,2048,768]{2,3,1,0:T(8,128)(2,1)} fusion(f32[768,2048]{1,0:T(8,128)} %fusion.64, bf16[640,768]{1,0:T(8,128)(2,1)S(1)} %copy-done.43, bf16[640,2048]{1,0:T(8,128)(2,1)S(1)} %copy-done.21), kind=kOutput, calls=%fused_computation.35 | convolution fusion | flops 2016411648 | bytes 13041664 | tf_op jit(solution)/shard_map/dot_general | solution.py:60
  (206 shorter events, 170.5 us)
Async XLA Ops:
  7.2 7.6 %copy-start.39 = (s32[1,8]{1,0:T(1,128)S(1)}, s32[1,8]{1,0:T(1,128)}, u32[]{:S(2)}) copy-start(s32[1,8]{1,0:T(1,128)} %param.11) | copy-start | bytes 100
  23.2 10.0 %copy-start.15 = (bf16[1,1,2048,768]{3,2,1,0:T(8,128)(2,1)S(1)}, bf16[1,1,2048,768]{3,2,1,0:T(8,128)(2,1)}, u32[]{:S(2)}) copy-start(bf16[1,1,2048,768]{3,2,1,0:T(8,128)(2,1)} %param.12) | copy-start | bytes 9437188
  23.2 69.1 %all-to-all-start = ((bf16[32,25,2048]{2,1,0:T(8,128)(2,1)}), bf16[32,25,2048]{2,1,0:T(8,128)(2,1)}, u32[]{:S(2)}, u32[]{:S(2)}) async-start(bf16[32,25,2048]{2,1,0:T(8,128)(2,1)} %reshape.671), calls=%async_computation | async-start | bytes 8388608 | tf_op jit(solution)/shard_map/all_to_all | solution.py:111
  31.8 221.7 %all-reduce.3.cloned.1.call-start = ((), (), s32[]{:S(2)}) async-start(), calls=%async_computation.8 | async-start | bytes 12582912 | tf_op jit(solution)/shard_map/psum | solution.py:92
  46.6 55.0 %copy-start.24 = (bf16[1,2,1,32,25,768]{5,3,4,2,1,0:T(8,128)(2,1)S(1)}, bf16[1,2,1,32,25,768]{5,3,4,2,1,0:T(8,128)(2,1)}, u32[]{:S(2)}) copy-start(bf16[1,2,1,32,25,768]{5,3,4,2,1,0:T(8,128)(2,1)} %param.15) | copy-start | bytes 7372804
  92.3 72.4 %all-to-all-start.2 = ((bf16[32,25,2048]{2,1,0:T(8,128)(2,1)}), bf16[32,25,2048]{2,1,0:T(8,128)(2,1)}, u32[]{:S(2)}, u32[]{:S(2)}) async-start(bf16[32,25,2048]{2,1,0:T(8,128)(2,1)} %reshape.678), calls=%async_computation.2 | async-start | bytes 8388608 | tf_op jit(solution)/shard_map/all_to_all | solution.py:111
  101.6 417.4 %reduce-scatter.3.cloned.1.call-start = ((), (), s32[]{:S(2)}) async-start(), calls=%async_computation.6 | async-start | bytes 7864320 | tf_op jit(solution)/shard_map/reduce_scatter | solution.py:171
  109.3 5.5 %copy-start.2 = (bf16[32,25,2048]{2,0,1:T(8,128)(2,1)}, bf16[32,25,2048]{2,0,1:T(8,128)(2,1)S(1)}, u32[]{:S(2)}) copy-start(bf16[32,25,2048]{2,0,1:T(8,128)(2,1)S(1)} %get-tuple-element.29) | copy-start | bytes 9830404
  256.5 5.7 %copy-start.28 = (f32[160,768]{1,0:T(8,128)}, f32[160,768]{1,0:T(8,128)S(1)}, u32[]{:S(2)}) copy-start(f32[160,768]{1,0:T(8,128)S(1)} %convolution_bitcast_fusion) | copy-start | bytes 1474564
  268.8 252.8 %reduce-scatter.5.cloned.1.call-start = ((), (), s32[]{:S(2)}) async-start(), calls=%async_computation.7 | async-start | bytes 7864320 | tf_op jit(solution)/shard_map/reduce_scatter | solution.py:171
  321.8 8.8 %copy-start.16 = (bf16[1,1,2048,768]{3,2,1,0:T(8,128)(2,1)S(1)}, bf16[1,1,2048,768]{3,2,1,0:T(8,128)(2,1)}, u32[]{:S(2)}) copy-start(bf16[1,1,2048,768]{3,2,1,0:T(8,128)(2,1)} %param.12) | copy-start | bytes 9437188
  349.5 70.8 %all-to-all-start.1 = ((bf16[32,25,2048]{2,1,0:T(8,128)(2,1)}), bf16[32,25,2048]{2,1,0:T(8,128)(2,1)}, u32[]{:S(2)}, u32[]{:S(2)}) async-start(bf16[32,25,2048]{2,1,0:T(8,128)(2,1)} %pad_maximum_fusion), calls=%async_computation.1 | async-start | bytes 8388608 | tf_op jit(solution)/shard_map/all_to_all | solution.py:151
  391.8 8.6 %copy-start.17 = (bf16[1,1,2048,768]{3,2,1,0:T(8,128)(2,1)S(1)}, bf16[1,1,2048,768]{3,2,1,0:T(8,128)(2,1)}, u32[]{:S(2)}) copy-start(bf16[1,1,2048,768]{3,2,1,0:T(8,128)(2,1)} %param.12) | copy-start | bytes 9437188
  404.2 5.2 copy-start.36
  417.8 8.9 %copy-start.3 = (bf16[640,2048]{1,0:T(8,128)(2,1)S(1)}, bf16[640,2048]{1,0:T(8,128)(2,1)}, u32[]{:S(2)}) copy-start(bf16[640,2048]{1,0:T(8,128)(2,1)} %reshape.684) | copy-start | bytes 7864324
  420.3 69.0 %all-to-all-start.3 = ((bf16[32,25,2048]{2,1,0:T(8,128)(2,1)}), bf16[32,25,2048]{2,1,0:T(8,128)(2,1)}, u32[]{:S(2)}, u32[]{:S(2)}) async-start(bf16[32,25,2048]{2,1,0:T(8,128)(2,1)} %pad_maximum_fusion.1), calls=%async_computation.3 | async-start | bytes 8388608 | tf_op jit(solution)/shard_map/all_to_all | solution.py:151
  426.7 5.9 %copy-start.22 = (bf16[640,2048]{1,0:T(8,128)(2,1)S(1)}, bf16[640,2048]{1,0:T(8,128)(2,1)}, u32[]{:S(2)}) copy-start(bf16[640,2048]{1,0:T(8,128)(2,1)} %reshape.672) | copy-start | bytes 7864324
  426.7 5.9 %copy-start.30 = (f32[640,768]{1,0:T(8,128)S(1)}, f32[640,768]{1,0:T(8,128)}, u32[]{:S(2)}) copy-start(f32[640,768]{1,0:T(8,128)} %reshape.693) | copy-start | bytes 5898244
  426.7 5.9 %copy-start.41 = (f32[640,768]{1,0:T(8,128)S(1)}, f32[640,768]{1,0:T(8,128)}, u32[]{:S(2)}) copy-start(f32[640,768]{1,0:T(8,128)} %fusion.5) | copy-start | bytes 5898244
  496.0 4.6 copy-start.25
  501.5 7.3 %copy-start.33 = (bf16[640,768]{1,0:T(8,128)(2,1)S(1)}, bf16[640,768]{1,0:T(8,128)(2,1)}, u32[]{:S(2)}) copy-start(bf16[640,768]{1,0:T(8,128)(2,1)} %get-tuple-element.32) | copy-start | bytes 2949124
  501.5 17.4 %collective-permute-start = (bf16[2,64,2048]{2,1,0:T(8,128)(2,1)}, bf16[2,64,2048]{2,1,0:T(8,128)(2,1)}, u32[]{:S(2)}, u32[]{:S(2)}) collective-permute-start(bf16[2,64,2048]{2,1,0:T(8,128)(2,1)} %pad_maximum_fusion.2), channel_id=1, source_target_pairs={{32,0},{64,32},{96,64},{0,96},{33,1},{65,33},{97,65},{1,97},{34,2}... | collective-permute-start | bytes 1572872 | tf_op jit(solution)/shard_map/ppermute | solution.py:20
  510.3 4.7 copy-start.38
  510.3 4.8 copy-start.37
  (29 other events, 69.9 us)
Sparse Core Ops, SparseCore 0:
  38.2 215.2 all-reduce.2
  269.0 63.8 reduce-scatter.2
  335.2 158.3 reduce-scatter.4
